TPU v7x, 32 devices: a whole 2x2x4 slice. The times are simulated.
32 devices in a mesh: groups: 2 (over y), blk: 4 (over z), pool: 4 (over x, core).
Axes of the slice: x: 2, y: 2, z: 4, core: 2. Of those that a mesh axis runs over, the one named last changes fastest.
Arguments:
- q_new: bfloat16 [1024, 8192], P(('groups', 'blk'), 'pool'), parts along dimension 0, may hold values from -64 to 64
- kv_new: bfloat16 [1024, 8, 256], P(('groups', 'blk'), 'pool'), parts along dimension 0, may hold values from -7 to 7
- kv_cache: bfloat16 [256, 8, 128, 256], P(('groups', 'blk'), 'pool'), parts along dimension 0, may hold values from -4.5 to 4.5
- page_table: int32 [16], P('groups'), parts along dimension 0, may hold values from 0 to 127, as said below
- block_offsets: int32 [8], P('groups'), parts along dimension 0, may hold values from 0 to 3, each once
Outputs:
- attended: bfloat16 [1024, 8192], P(('groups', 'blk'), 'pool'), parts along dimension 0
There are 2 independent parts, one for each index of `groups`. A program takes and returns all parts, laid end to end along the dimension named above; each array names one. Nothing has to cross between parts.
Inputs may be any that keep to these rules, and one draw needn't show every extreme that they name: `page_table`: distinct slots; slot s lies on blk index s // 32; at most 4 entries lie on the slots of one blk index, and exactly 4 on some blk index.
All inputs are finite; a program needn't handle non-finite values.
Results may differ from a plain program's by a relative error of at most 0.0045.
Values may be sent and summed in bfloat16 or wider, within the bound.
No kernel may reach another device: no remote copies, remote signals or barrier semaphores. Data moves between devices by JAX's collectives and lax.ppermute only.
A program may use at most 64 MiB of HBM per device.

v0:
```python
import math
import jax
import jax.numpy as jnp
from jax import lax
from jax.sharding import PartitionSpec as P

CAP = 4


def attend(running, queries, keys, values, visible, head_size):
    maxima, totals, summed = running
    score_scale = 1.0 / math.sqrt(head_size)
    scores = (
        jnp.einsum("gqd,gkd->gqk", queries, keys, preferred_element_type=jnp.float32) * score_scale
    )
    scores = jnp.where(visible, scores, -1e30)
    row_top = jnp.maximum(maxima, jnp.max(scores, axis=2))
    factor = jnp.exp(maxima - row_top)
    weights = jnp.where(visible, jnp.exp(scores - row_top[..., None]), 0.0)
    totals = totals * factor + jnp.sum(weights, axis=2)
    summed = summed * factor[..., None] + jnp.einsum(
        "gqk,gkd->gqd", weights.astype(jnp.bfloat16), values, preferred_element_type=jnp.float32
    )
    return (row_top, totals, summed)


def local(q_new, kv_new, kv_cache, page_table, block_offsets):
    q_rows = q_new.shape[0]
    kv_heads = kv_new.shape[1]
    head_size = kv_new.shape[2] // 2
    group_size = q_new.shape[1] // (head_size * kv_heads)
    slots_dev = kv_cache.shape[0]
    page_len = kv_cache.shape[2]
    npages = page_table.shape[0]
    blocks = lax.axis_size("blk")
    myself = lax.axis_index("blk")
    pg = -(-npages // blocks)
    block_ids = jnp.arange(blocks, dtype=jnp.int32)
    my_offset = jnp.sum(jnp.where(block_ids == myself, block_offsets, 0))
    query_pos = jnp.tile(my_offset * q_rows + jnp.arange(q_rows, dtype=jnp.int32), group_size)
    queries = (
        q_new.reshape(q_rows, kv_heads, group_size, head_size)
        .transpose(1, 2, 0, 3)
        .reshape(kv_heads, group_size * q_rows, head_size)
    )
    query_span = group_size * q_rows
    new_all = lax.all_gather(kv_new.transpose(1, 0, 2), "blk", axis=0)
    page_owner = page_table // slots_dev
    owned = page_owner == myself
    page_rank = jnp.cumsum(owned.astype(jnp.int32)) - 1
    local_slot = page_table % slots_dev
    counts = jnp.sum((page_owner[None, :] == block_ids[:, None]).astype(jnp.int32), axis=1)
    per_peer = (CAP + blocks - 1) // blocks
    starts = jnp.cumsum(counts) - counts
    my_start = jnp.sum(jnp.where(block_ids == myself, starts, 0))
    peer_slots = jnp.arange(per_peer, dtype=jnp.int32)[None, :]
    wanted = (block_ids[:, None] - my_start) % blocks + peer_slots * blocks
    picked = owned[None, None, :] & (page_rank[None, None, :] == wanted[..., None])
    chosen = jnp.sum(jnp.where(picked, local_slot[None, None, :], 0), axis=2).reshape(-1)
    sent_pages = kv_cache[chosen].reshape(blocks, per_peer, kv_heads, page_len, 2 * head_size)
    sent_pages = sent_pages.transpose(0, 2, 1, 3, 4).reshape(
        blocks, kv_heads, per_peer * page_len, 2 * head_size
    )
    received = lax.all_to_all(sent_pages, "blk", split_axis=0, concat_axis=0, tiled=True)
    page_part = received[:, :, : per_peer * page_len]
    page_part = page_part.reshape(blocks, kv_heads, per_peer, page_len, 2 * head_size)
    page_part = page_part.transpose(0, 2, 1, 3, 4).reshape(
        blocks * per_peer, kv_heads, page_len, 2 * head_size
    )
    arriving = (myself - starts[:, None]) % blocks + peer_slots * blocks
    present = (arriving < counts[:, None]).reshape(-1)
    order_rank = jnp.cumsum(present.astype(jnp.int32)) - 1
    choose = present[None, :] & (order_rank[None, :] == jnp.arange(pg, dtype=jnp.int32)[:, None])
    positions = jnp.sum(
        jnp.where(choose, jnp.arange(blocks * per_peer, dtype=jnp.int32)[None, :], 0), axis=1
    )
    compact = page_part[positions]
    compact_valid = jnp.arange(pg, dtype=jnp.int32) * blocks + myself < npages
    gathered = lax.all_gather(compact, "blk", axis=0, tiled=True)
    gathered_valid = (
        jnp.arange(pg, dtype=jnp.int32)[None, :] * blocks + block_ids[:, None] < npages
    ).reshape(-1)
    new_rows = new_all.transpose(1, 0, 2, 3).reshape(kv_heads, blocks * q_rows, 2 * head_size)
    own_pages = compact.transpose(1, 0, 2, 3).reshape(kv_heads, pg * page_len, 2 * head_size)
    entries_a = jnp.concatenate([new_rows, own_pages], axis=1)
    row_source = jnp.repeat(block_ids, q_rows)
    key_pos = jnp.sum(
        jnp.where(row_source[:, None] == block_ids[None, :], block_offsets[None, :], 0), axis=1
    ) * q_rows + jnp.tile(jnp.arange(q_rows, dtype=jnp.int32), blocks)
    visible_new = key_pos[None, :] <= query_pos[:, None]
    visible_own = jnp.broadcast_to(
        jnp.repeat(compact_valid, page_len)[None, :], (query_span, pg * page_len)
    )
    visible_a = jnp.concatenate([visible_new, visible_own], axis=1)[None]
    running = (
        jnp.full((kv_heads, query_span), -1e30, jnp.float32),
        jnp.zeros((kv_heads, query_span), jnp.float32),
        jnp.zeros((kv_heads, query_span, head_size), jnp.float32),
    )
    running = attend(
        running,
        queries,
        entries_a[..., :head_size],
        entries_a[..., head_size:],
        visible_a,
        head_size,
    )
    page_block = jnp.repeat(block_ids, pg)
    use_page = gathered_valid & (page_block != myself)
    entries_b = gathered.transpose(1, 0, 2, 3).reshape(
        kv_heads, blocks * pg * page_len, 2 * head_size
    )
    visible_b = jnp.repeat(use_page, page_len)[None, None, :]
    running = attend(
        running,
        queries,
        entries_b[..., :head_size],
        entries_b[..., head_size:],
        visible_b,
        head_size,
    )
    maxima, totals, summed = running
    attended = (summed / totals[..., None]).astype(jnp.bfloat16)
    attended = attended.reshape(kv_heads, group_size, q_rows, head_size).transpose(2, 0, 1, 3)
    return attended.reshape(q_rows, kv_heads * group_size * head_size)


def solution(mesh):
    return jax.shard_map(
        local,
        mesh=mesh,
        in_specs=(
            P(("groups", "blk"), "pool"),
            P(("groups", "blk"), "pool", None),
            P(("groups", "blk"), "pool", None, None),
            P("groups"),
            P("groups"),
        ),
        out_specs=P(("groups", "blk"), "pool"),
        check_vma=False,
    )
```

profile of v0, /device:TPU:0, one launch (start us, length us, event | category | flops | bytes accessed | tf_op | source)
XLA Modules:
  0.0 99.0 jit_solution(9851125789988168862)
XLA Ops:
  6.5 0.7 and_select_fusion.3
  7.2 0.7 convert_bitcast_fusion
  7.9 0.2 reduce-window.21
  8.1 0.1 convert_reduce_fusion
  8.2 0.2 reduce-window.22
  8.3 1.4 %fusion.35 = (s32[]{:T(128)}, s32[]{:T(128)}) fusion(s32[4]{0:T(128)} %param.9, s32[]{:T(128)S(6)} %axis_index.15, s32[4]{0:T(128)S(1)} %convert_reduce_fusion, s32[4,1]{0,1:T(1,128)S(1)} %reduce-window.22), kind=kLoop, calls=%fused_computation.77 | loop fusion | flops 22 | bytes 60 | tf_op jit(solution)/shard_map/reduce_sum | solution.py:39
  9.7 0.7 and_select_fusion.4
  10.4 0.2 select_reduce_fusion.1
  10.6 3.6 %gather_fusion = bf16[4,2,128,256]{3,2,1,0:T(8,128)(2,1)} fusion(bf16[32,2,128,256]{3,2,1,0:T(8,128)(2,1)} %param.7, s32[1024]{0:T(1024)S(1)} %pad_clamp_fusion.1), kind=kCustom, calls=%fused_computation | custom fusion | bytes 1048592 | tf_op jit(solution)/shard_map/gather | solution.py:60
  14.1 6.3 %all-to-all-start = ((bf16[4,2,128,256]{3,2,1,0:T(8,128)(2,1)}), bf16[4,2,128,256]{3,2,1,0:T(8,128)(2,1)S(1)}, u32[]{:S(2)}, u32[]{:S(2)}) async-start(bf16[4,2,128,256]{3,2,1,0:T(8,128)(2,1)} %gather_fusion), calls=%async_computation | async-start | bytes 1048576 | tf_op jit(solution)/shard_map/all_to_all | solution.py:64
  20.5 0.0 all-gather.4.cloned.1.call-start
  20.5 0.1 broadcast_bitcast_fusion.2
  20.6 0.1 and.99
  21.4 0.2 reduce-window.23
  21.6 0.9 copy.36
  22.5 22.7 %all-gather = bf16[8,128,256]{2,1,0:T(8,128)(2,1)S(1)} all-gather(bf16[2,128,256]{2,1,0:T(8,128)(2,1)S(1)} %bitcast.101), channel_id=2, replica_groups=mesh['groups'=2,'blk'=4,'pool'=4] {'blk'}, dimensions={0}, use_global_device_ids=true | all-gather | bytes 655360 | tf_op jit(solution)/shard_map/all_gather | solution.py:47
  45.3 1.1 %copy.31 = bf16[16,8,16,128]{3,2,1,0:T(8,128)(2,1)S(1)} copy(bf16[16,8,16,128]{3,1,2,0:T(8,128)(2,1)} %bitcast.102) | data formatting | bytes 1048576
  46.4 0.1 copy.24
  46.6 0.1 fusion.33
  46.8 0.7 select_reduce_fusion
  47.5 0.0 all-to-all-done
  47.5 1.3 %gather_fusion.1 = bf16[2,2,128,256]{3,2,1,0:T(8,128)(2,1)} fusion(bf16[4,2,128,256]{3,2,1,0:T(8,128)(2,1)S(1)} %all-to-all-done, s32[1024]{0:T(1024)S(1)} %pad_clamp_fusion), kind=kCustom, calls=%fused_computation.1 | custom fusion | bytes 524296 | tf_op jit(solution)/shard_map/gather | solution.py:77
  48.8 0.0 all-gather.4.cloned.1.call-update
  48.8 0.1 broadcast_bitcast_fusion.1
  48.9 0.4 broadcast_compare_fusion
  49.2 0.4 pad_add_fusion
  49.7 1.0 copy.23
  50.6 4.0 %fusion.4 = (f32[2,1024]{1,0:T(2,128)S(1)}, f32[2,768,1024]{2,1,0:T(8,128)}) fusion(pred[1024,768]{0,1:T(8,128)(4,1)S(1)} %pad_add_fusion, bf16[2,1024,128]{2,1,0:T(8,128)(2,1)S(1)} %bitcast.95, bf16[2,512,256]{2,1,0:T(8,128)(2,1)S(1)} %bitcast.103, bf16[2,256,256]{2,1,0:T(8,128)(2,1)S(1)} %bitcast.106), kind=kOutput, calls=%fused_computation.11 | convolution fusion | flops 408156160 | bytes 8396800 | tf_op jit(solution)/shard_map/gqd,gkd->gqk/dot_general | solution.py:14
  54.7 23.0 %all-gather.4.cloned.1.call-done = bf16[8,2,128,256]{3,2,1,0:T(8,128)(2,1)} async-done(((bf16[2,2,128,256]{3,2,1,0:T(8,128)(2,1)}), bf16[8,2,128,256]{3,2,1,0:T(8,128)(2,1)}) %all-gather.4.cloned.1.call-update) | async-done | bytes 1048592 | tf_op jit(solution)/shard_map/all_gather | solution.py:79
  77.7 1.3 %copy.26 = bf16[2,8,128,256]{3,2,1,0:T(8,128)(2,1)S(1)} copy(bf16[2,8,128,256]{3,2,0,1:T(8,128)(2,1)} %bitcast.100) | data formatting | bytes 2097152 | tf_op jit(solution)/shard_map/transpose | solution.py:110
  79.0 0.0 slice-start
  79.0 0.0 slice-start.1
  79.0 1.9 %bitcast_reduce_fusion = (f32[2,1024]{1,0:T(2,128)S(1)}, f32[2,1024,1024]{2,1,0:T(8,128)S(1)}) fusion(pred[1024]{0:T(1024)(128)(4,1)S(1)} %broadcast_bitcast_fusion.1, bf16[2,1024,128]{2,1,0:T(8,128)(2,1)S(1)} %bitcast.96, bf16[2,1024,256]{2,1,0:T(8,128)(2,1)S(1)} %bitcast.92), kind=kOutput, calls=%fused_computation.3 | convolution fusion | flops 543160320 | bytes 9446400 | tf_op jit(solution)/shard_map/gqd,gkd->gqk/dot_general | solution.py:14
  80.9 2.5 %fusion.2 = f32[2,1024]{1,0:T(2,128)S(1)} fusion(f32[2,1024,1024]{2,1,0:T(8,128)S(1)} %get-tuple-element.16, f32[2,1024]{1,0:T(2,128)S(1)} %get-tuple-element.11, pred[1024]{0:T(1024)(128)(4,1)S(1)} %broadcast_bitcast_fusion.1), kind=kLoop, calls=%fused_computation.9 | loop fusion | flops 10483712 | bytes 8406016 | tf_op jit(solution)/shard_map/reduce_sum | solution.py:20
  83.4 0.0 slice-done
  83.4 0.0 slice-done.1
  83.5 1.7 %fusion.5 = f32[2,1024]{1,0:T(2,128)S(1)} fusion(f32[2,768,1024]{2,1,0:T(8,128)S(1)} %bitcast.91, f32[2,1024]{1,0:T(2,128)S(1)} %get-tuple-element.12, pred[1024,768]{0,1:T(8,128)(4,1)S(1)} %pad_add_fusion), kind=kLoop, calls=%fused_computation.12 | loop fusion | flops 7862272 | bytes 7094272 | tf_op jit(solution)/shard_map/reduce_sum | solution.py:20
  85.1 2.8 %fusion.20 = f32[2,1024,128]{2,1,0:T(8,128)S(1)} fusion(f32[2,768,1024]{2,1,0:T(8,128)S(1)} %bitcast.91, f32[2,1024]{1,0:T(2,128)S(1)} %get-tuple-element.12, pred[1024,768]{0,1:T(8,128)(4,1)S(1)} %pad_add_fusion, f32[2,1024]{1,0:T(2,128)S(1)} %get-tuple-element.6, f32[2,1024]{1,0:T(2,128)S(1)} %get-tuple-element.10, ...), kind=kOutput, calls=%fused_computation.22 | convolution fusion | flops 411828224 | bytes 8937472 | tf_op jit(solution)/shard_map/gqk,gkd->gqd/dot_general | solution.py:21
  88.0 3.0 %divide_convert_fusion = bf16[2,1024,128]{2,1,0:T(8,128)(2,1)S(1)} fusion(f32[2,1024,128]{2,1,0:T(8,128)S(1)} %fusion.20, f32[2,1024,1024]{2,1,0:T(8,128)S(1)} %get-tuple-element.16, f32[2,1024]{1,0:T(2,128)S(1)} %get-tuple-element.11, pred[1024]{0:T(1024)(128)(4,1)S(1)} %broadcast_bitcast_fusion.1, bf16[2,1024,256]{2,1,0:T(8,128)(2,1)S(1)} %bitcast.93, ...), kind=kOutput, calls=%fused_computation.23 | convolution fusion | flops 548143104 | bytes 10504192 | tf_op jit(solution)/shard_map/gqk,gkd->gqd/dot_general | solution.py:21
  90.9 0.3 copy.28
  91.3 0.9 copy.35
  (20 shorter events, 0.2 us)
Async XLA Ops:
  14.1 33.4 %all-to-all-start = ((bf16[4,2,128,256]{3,2,1,0:T(8,128)(2,1)}), bf16[4,2,128,256]{3,2,1,0:T(8,128)(2,1)S(1)}, u32[]{:S(2)}, u32[]{:S(2)}) async-start(bf16[4,2,128,256]{3,2,1,0:T(8,128)(2,1)} %gather_fusion), calls=%async_computation | async-start | bytes 1048576 | tf_op jit(solution)/shard_map/all_to_all | solution.py:64
  20.5 57.2 %all-gather.4.cloned.1.call-start = ((), (), s32[]{:S(2)}) async-start(), calls=%async_computation.1 | async-start | bytes 1310720 | tf_op jit(solution)/shard_map/all_gather | solution.py:79
  79.0 4.4 %slice-start = ((s8[6291456]{0:T(1024)(128)(4,1)}), s8[4194304]{0:T(1024)(128)(4,1)S(1)}, s32[]{:S(2)}) async-start(s8[6291456]{0:T(1024)(128)(4,1)} %bitcast.90), calls=%async_computation.2 | async-start | bytes 8388608
  79.0 4.4 %slice-start.1 = ((s8[6291456]{0:T(1024)(128)(4,1)}), s8[2097152]{0:T(1024)(128)(4,1)S(1)}, s32[]{:S(2)}) async-start(s8[6291456]{0:T(1024)(128)(4,1)} %bitcast.90), calls=%async_computation.3 | async-start | bytes 4194304
Sparse Core Ops, SparseCore 0:
  48.9 28.7 all-gather.3
where the time goes:
time: 99.4 us; the launch traced here: 99 us
  waiting for transfers between devices  23.1 us (23%)
  blocking collectives  22.7 us (23%)
  between operations  14.3 us (14%)
  matrix products  11.7 us (12%)
  local copies, waits for them, and re-layouts  10.9 us (11%)
  other arithmetic  10.1 us (10%)
  starting transfers between devices  6.32 us (6%)
    all_gather x1, waiting for transfers between devices, local(): gathered = lax.all_gather(compact, 'blk', axis=0, tiled=True)  23 us
    all_gather x1, blocking collectives, local(): new_all = lax.all_gather(kv_new.transpose(1, 0, 2), 'blk', axis=0)  22.7 us
    all_to_all x1, starting transfers between devices, local(): lax.all_to_all(sent_pages, 'blk', split_axis=0, concat_axis=0, tiled=True)  6.32 us
    dot_general x2, matrix products, attend(): jnp.einsum('gqd,gkd->gqk', queries, keys, preferred_element_type=jnp.floa...  5.92 us
    dot_general x2, matrix products, attend(): jnp.einsum('gqk,gkd->gqd', weights.astype(jnp.bfloat16), values, preferre...  5.77 us
    reduce_sum x2, other arithmetic, attend(): totals = totals * factor + jnp.sum(weights, axis=2)  4.12 us
    gather x1, local copies, waits for them, and re-layouts, local(): kv_cache[chosen]  3.56 us
    unnamed x7, local copies, waits for them, and re-layouts  3.01 us
  transfers between devices with their start and end apart: 2, of which 1 were waited for; matrix products, arithmetic and copies ran while one was open for 9% of the time, Pallas kernels for 0%

commit v1 on v0

--- a/solution.py
+++ b/solution.py
@@ -76,7 +76,16 @@
     )
     compact = page_part[positions]
     compact_valid = jnp.arange(pg, dtype=jnp.int32) * blocks + myself < npages
-    gathered = lax.all_gather(compact, "blk", axis=0, tiled=True)
+    axis_len = lax.axis_size("blk")
+    u_next = [(hop_no - 1, hop_no) for hop_no in range(1, axis_len)] + [(axis_len - 1, 0)]
+    plain = compact
+    sheets = [plain]
+    for _ in range(axis_len - 1):
+        plain = lax.ppermute(plain, "blk", u_next)
+        sheets += [plain]
+    mid_arr = jnp.concatenate([*reversed(sheets)], 0)
+    w2 = lax.axis_index("blk")
+    gathered = jnp.roll(mid_arr, (w2 + 1) * plain.shape[0], 0)
     gathered_valid = (
         jnp.arange(pg, dtype=jnp.int32)[None, :] * blocks + block_ids[:, None] < npages
     ).reshape(-1)

time: 99.4 us -> 84.5 us (0.85)
  between operations: 14.3 us -> 0.96 us
  waiting for transfers between devices: 23.1 us -> 27.9 us
  local copies, waits for them, and re-layouts: 10.9 us -> 8.24 us
  matrix products: 11.7 us -> 9.36 us
  blocking collectives: 22.7 us -> 21.1 us
    all_gather x1 -> x0, waiting for transfers between devices: 23 us -> none  [local(): gathered = lax.all_gather(compact, 'blk', axis=0, tiled=True)]
    ppermute x0 -> x3, waiting for transfers between devices: none -> 16.4 us  [local(): plain = lax.ppermute(plain, 'blk', u_next)]
    all_to_all x1, waiting for transfers between devices: 0.01 us -> 11.5 us  [local(): lax.all_to_all(sent_pages, 'blk', split_axis=0, concat_axis=0, tiled=True)]
    dot_general x2, matrix products: 5.92 us -> 3.27 us  [attend(): jnp.einsum('gqd,gkd->gqk', queries, keys, preferred_element_type=jnp.floa...]
    all_gather x1, blocking collectives: 22.7 us -> 21.1 us  [local(): new_all = lax.all_gather(kv_new.transpose(1, 0, 2), 'blk', axis=0)]
    transpose x1 -> x2, local copies, waits for them, and re-layouts: 1.29 us -> 0.18 us  [local(): gathered.transpose(1, 0, 2, 3)]
    unnamed x7 -> x10, local copies, waits for them, and re-layouts: 3.01 us -> 3.14 us
  transfers between devices with their start and end apart: 2 -> 4, of which waited for: 1 -> 3; matrix products, arithmetic and copies ran while one was open for 9% -> 7% of each run, Pallas kernels for 0% -> 0%
where the time goes in v1:
time: 84.5 us; the launch traced here: 84.2 us
  waiting for transfers between devices  27.9 us (33%)
  blocking collectives  21.1 us (25%)
  other arithmetic  10.2 us (12%)
  matrix products  9.36 us (11%)
  local copies, waits for them, and re-layouts  8.24 us (10%)
  starting transfers between devices  6.44 us (8%)
  between operations  0.96 us (1%)
    all_gather x1, blocking collectives, local(): new_all = lax.all_gather(kv_new.transpose(1, 0, 2), 'blk', axis=0)  21.1 us
    ppermute x3, waiting for transfers between devices, local(): plain = lax.ppermute(plain, 'blk', u_next)  16.4 us
    all_to_all x1, waiting for transfers between devices, local(): lax.all_to_all(sent_pages, 'blk', split_axis=0, concat_axis=0, tiled=True)  11.5 us
    all_to_all x1, starting transfers between devices, local(): lax.all_to_all(sent_pages, 'blk', split_axis=0, concat_axis=0, tiled=True)  6.32 us
    dot_general x2, matrix products, attend(): jnp.einsum('gqk,gkd->gqd', weights.astype(jnp.bfloat16), values, preferre...  6.09 us
    reduce_sum x2, other arithmetic, attend(): totals = totals * factor + jnp.sum(weights, axis=2)  4.19 us
    gather x1, local copies, waits for them, and re-layouts, local(): kv_cache[chosen]  3.56 us
    dot_general x2, matrix products, attend(): jnp.einsum('gqd,gkd->gqk', queries, keys, preferred_element_type=jnp.floa...  3.27 us
  transfers between devices with their start and end apart: 4, of which 3 were waited for; matrix products, arithmetic and copies ran while one was open for 7% of the time, Pallas kernels for 0%

profile of v1, /device:TPU:0, one launch (start us, length us, event | category | flops | bytes accessed | tf_op | source)
XLA Modules:
  0.0 84.2 jit_solution(504096796173088529)
XLA Ops:
  0.0 0.7 and_select_fusion.3
  0.7 0.7 convert_bitcast_fusion
  1.3 0.2 reduce-window.21
  1.5 0.1 convert_reduce_fusion
  1.6 0.2 reduce-window.22
  1.8 1.4 %fusion.35 = (s32[]{:T(128)}, s32[]{:T(128)}) fusion(s32[4]{0:T(128)} %param.9, s32[]{:T(128)S(6)} %axis_index.19, s32[4]{0:T(128)S(1)} %convert_reduce_fusion, s32[4,1]{0,1:T(1,128)S(1)} %reduce-window.22), kind=kLoop, calls=%fused_computation.86 | loop fusion | flops 22 | bytes 60 | tf_op jit(solution)/shard_map/reduce_sum | solution.py:39
  3.2 0.7 and_select_fusion.4
  3.8 0.2 select_reduce_fusion.1
  4.1 3.6 %gather_fusion = bf16[4,2,128,256]{3,2,1,0:T(8,128)(2,1)} fusion(bf16[32,2,128,256]{3,2,1,0:T(8,128)(2,1)} %param.7, s32[1024]{0:T(1024)S(1)} %pad_clamp_fusion.1), kind=kCustom, calls=%fused_computation | custom fusion | bytes 1048592 | tf_op jit(solution)/shard_map/gather | solution.py:60
  7.6 6.3 %all-to-all-start = ((bf16[4,2,128,256]{3,2,1,0:T(8,128)(2,1)}), bf16[4,2,128,256]{3,2,1,0:T(8,128)(2,1)S(1)}, u32[]{:S(2)}, u32[]{:S(2)}) async-start(bf16[4,2,128,256]{3,2,1,0:T(8,128)(2,1)} %gather_fusion), calls=%async_computation | async-start | bytes 1048576 | tf_op jit(solution)/shard_map/all_to_all | solution.py:64
  14.0 0.1 broadcast_bitcast_fusion.2
  14.1 0.2 reduce-window.23
  14.3 0.1 fusion.33
  15.1 0.1 and.105
  15.2 0.9 %copy.36 = bf16[128,2,256]{2,0,1:T(8,128)(2,1)S(1)} copy(bf16[128,2,256]{2,1,0:T(2,128)(2,1)} %param.6) | data formatting | bytes 262144 | tf_op args[1]
  16.1 0.7 select_reduce_fusion
  16.9 0.1 broadcast_bitcast_fusion.1
  16.9 11.5 %all-to-all-done = bf16[4,2,128,256]{3,2,1,0:T(8,128)(2,1)S(1)} async-done(((bf16[4,2,128,256]{3,2,1,0:T(8,128)(2,1)}), bf16[4,2,128,256]{3,2,1,0:T(8,128)(2,1)S(1)}, u32[]{:S(2)}, u32[]{:S(2)}) %all-to-all-start) | async-done | bytes 524320 | tf_op jit(solution)/shard_map/all_to_all | solution.py:64
  28.4 0.6 gather_fusion.1
  29.0 0.1 collective-permute-start
  29.1 21.1 %all-gather = bf16[8,128,256]{2,1,0:T(8,128)(2,1)S(1)} all-gather(bf16[2,128,256]{2,1,0:T(8,128)(2,1)S(1)} %bitcast.99), channel_id=2, replica_groups=mesh['groups'=2,'blk'=4,'pool'=4] {'blk'}, dimensions={0}, use_global_device_ids=true | all-gather | bytes 655360 | tf_op jit(solution)/shard_map/all_gather | solution.py:47
  50.2 1.1 %copy.31 = bf16[16,8,16,128]{3,2,1,0:T(8,128)(2,1)S(1)} copy(bf16[16,8,16,128]{3,1,2,0:T(8,128)(2,1)} %bitcast.100) | data formatting | bytes 1048576
  51.4 0.1 copy.24
  51.5 0.4 broadcast_compare_fusion
  51.9 0.0 collective-permute-done
  51.9 0.1 collective-permute-start.1
  52.0 0.4 pad_add_fusion
  52.4 9.7 %collective-permute-done.1 = bf16[2,2,128,256]{3,2,1,0:T(8,128)(2,1)S(1)} collective-permute-done((bf16[2,2,128,256]{3,2,1,0:T(8,128)(2,1)S(1)}, bf16[2,2,128,256]{3,2,1,0:T(8,128)(2,1)S(1)}, u32[]{:S(2)}, u32[]{:S(2)}) %collective-permute-start.1) | collective-permute-done | bytes 262176 | tf_op jit(solution)/shard_map/ppermute | solution.py:84
  62.1 0.0 collective-permute-start.2
  62.1 1.4 %fusion.4 = (f32[2,1024]{1,0:T(2,128)S(1)}, f32[2,768,1024]{2,1,0:T(8,128)S(1)}) fusion(pred[1024,768]{0,1:T(8,128)(4,1)S(1)} %pad_add_fusion, bf16[2,1024,128]{2,1,0:T(8,128)(2,1)S(1)} %bitcast.94, bf16[2,512,256]{2,1,0:T(8,128)(2,1)S(1)} %bitcast.101, bf16[2,256,256]{2,1,0:T(8,128)(2,1)S(1)} %bitcast.104), kind=kOutput, calls=%fused_computation.11 | convolution fusion | flops 408156160 | bytes 8396800 | tf_op jit(solution)/shard_map/gqd,gkd->gqk/dot_general | solution.py:14
  63.5 6.8 %collective-permute-done.2 = bf16[2,2,128,256]{3,2,1,0:T(8,128)(2,1)S(1)} collective-permute-done((bf16[2,2,128,256]{3,2,1,0:T(8,128)(2,1)S(1)}, bf16[2,2,128,256]{3,2,1,0:T(8,128)(2,1)S(1)}, u32[]{:S(2)}, u32[]{:S(2)}) %collective-permute-start.2) | collective-permute-done | bytes 262176 | tf_op jit(solution)/shard_map/ppermute | solution.py:84
  70.5 0.1 dynamic-slice_bitcast_fusion
  70.6 0.1 copy.26
  70.7 1.9 %bitcast_reduce_fusion = (f32[2,1024]{1,0:T(2,128)S(1)}, f32[2,1024,1024]{2,1,0:T(8,128)S(1)}) fusion(pred[1024]{0:T(1024)(128)(4,1)S(1)} %broadcast_bitcast_fusion.1, bf16[2,1024,128]{2,1,0:T(8,128)(2,1)S(1)} %bitcast.95, bf16[2,1024,256]{2,1,0:T(8,128)(2,1)S(1)} %bitcast.92), kind=kOutput, calls=%fused_computation.3 | convolution fusion | flops 543160320 | bytes 9446400 | tf_op jit(solution)/shard_map/gqd,gkd->gqk/dot_general | solution.py:14
  72.6 2.5 %fusion.2 = f32[2,1024]{1,0:T(2,128)S(1)} fusion(f32[2,1024,1024]{2,1,0:T(8,128)S(1)} %get-tuple-element.16, f32[2,1024]{1,0:T(2,128)S(1)} %get-tuple-element.11, pred[1024]{0:T(1024)(128)(4,1)S(1)} %broadcast_bitcast_fusion.1), kind=kLoop, calls=%fused_computation.9 | loop fusion | flops 10483712 | bytes 8406016 | tf_op jit(solution)/shard_map/reduce_sum | solution.py:20
  75.1 1.7 %fusion.5 = f32[2,1024]{1,0:T(2,128)S(1)} fusion(f32[2,768,1024]{2,1,0:T(8,128)S(1)} %get-tuple-element.14, f32[2,1024]{1,0:T(2,128)S(1)} %get-tuple-element.12, pred[1024,768]{0,1:T(8,128)(4,1)S(1)} %pad_add_fusion), kind=kLoop, calls=%fused_computation.12 | loop fusion | flops 7862272 | bytes 7094272 | tf_op jit(solution)/shard_map/reduce_sum | solution.py:20
  76.8 2.9 %fusion.20 = f32[2,1024,128]{2,1,0:T(8,128)S(1)} fusion(f32[2,768,1024]{2,1,0:T(8,128)S(1)} %get-tuple-element.14, f32[2,1024]{1,0:T(2,128)S(1)} %get-tuple-element.12, pred[1024,768]{0,1:T(8,128)(4,1)S(1)} %pad_add_fusion, f32[2,1024]{1,0:T(2,128)S(1)} %get-tuple-element.6, f32[2,1024]{1,0:T(2,128)S(1)} %get-tuple-element.10, ...), kind=kOutput, calls=%fused_computation.22 | convolution fusion | flops 411828224 | bytes 8937472 | tf_op jit(solution)/shard_map/gqk,gkd->gqd/dot_general | solution.py:21
  79.8 3.1 %divide_convert_fusion = bf16[2,1024,128]{2,1,0:T(8,128)(2,1)S(1)} fusion(f32[2,1024,128]{2,1,0:T(8,128)S(1)} %fusion.20, f32[2,1024,1024]{2,1,0:T(8,128)S(1)} %get-tuple-element.16, f32[2,1024]{1,0:T(2,128)S(1)} %get-tuple-element.11, pred[1024]{0:T(1024)(128)(4,1)S(1)} %broadcast_bitcast_fusion.1, bf16[2,1024,256]{2,1,0:T(8,128)(2,1)S(1)} %bitcast.93, ...), kind=kOutput, calls=%fused_computation.23 | convolution fusion | flops 548143104 | bytes 10504192 | tf_op jit(solution)/shard_map/gqk,gkd->gqd/dot_general | solution.py:21
  82.9 0.3 copy.28
  83.3 0.9 %copy.35 = bf16[16,8,16,128]{3,1,2,0:T(8,128)(2,1)} copy(bf16[16,8,16,128]{3,2,1,0:T(8,128)(2,1)S(1)} %bitcast.97) | data formatting | bytes 1048576
  (28 shorter events, 0.4 us)
Async XLA Ops:
  7.6 20.8 %all-to-all-start = ((bf16[4,2,128,256]{3,2,1,0:T(8,128)(2,1)}), bf16[4,2,128,256]{3,2,1,0:T(8,128)(2,1)S(1)}, u32[]{:S(2)}, u32[]{:S(2)}) async-start(bf16[4,2,128,256]{3,2,1,0:T(8,128)(2,1)} %gather_fusion), calls=%async_computation | async-start | bytes 1048576 | tf_op jit(solution)/shard_map/all_to_all | solution.py:64
  29.0 22.9 %collective-permute-start = (bf16[2,2,128,256]{3,2,1,0:T(8,128)(2,1)S(1)}, bf16[2,2,128,256]{3,2,1,0:T(8,128)(2,1)S(1)}, u32[]{:S(2)}, u32[]{:S(2)}) collective-permute-start(bf16[2,2,128,256]{3,2,1,0:T(8,128)(2,1)S(1)} %gather_fusion.1), channel_id=1, source_target_pairs={{0,4},{4,8},{8,12},{12,0},{1,5},{5,9},{9,13},{13,1},{2,6},{6,10},{... | collective-permute-start | bytes 786440 | tf_op jit(solution)/shard_map/ppermute | solution.py:84
  51.9 10.2 %collective-permute-start.1 = (bf16[2,2,128,256]{3,2,1,0:T(8,128)(2,1)S(1)}, bf16[2,2,128,256]{3,2,1,0:T(8,128)(2,1)S(1)}, u32[]{:S(2)}, u32[]{:S(2)}) collective-permute-start(bf16[2,2,128,256]{3,2,1,0:T(8,128)(2,1)S(1)} %collective-permute-done), channel_id=1, source_target_pairs={{0,4},{4,8},{8,12},{12,0},{1,5},{5,9},{9,13},{13,1},{2,6},{6,10},{... | collective-permute-start | bytes 786440 | tf_op jit(solution)/shard_map/ppermute | solution.py:84
  62.1 8.2 %collective-permute-start.2 = (bf16[2,2,128,256]{3,2,1,0:T(8,128)(2,1)S(1)}, bf16[2,2,128,256]{3,2,1,0:T(8,128)(2,1)S(1)}, u32[]{:S(2)}, u32[]{:S(2)}) collective-permute-start(bf16[2,2,128,256]{3,2,1,0:T(8,128)(2,1)S(1)} %collective-permute-done.1), channel_id=1, source_target_pairs={{0,4},{4,8},{8,12},{12,0},{1,5},{5,9},{9,13},{13,1},{2,6},{6,10},{... | collective-permute-start | bytes 786440 | tf_op jit(solution)/shard_map/ppermute | solution.py:84
